TPU v7x, 32 devices: a whole 2x2x4 slice. The times are simulated.
32 devices in a mesh: dp: 4 (over y, x), ctx: 8 (over z, core).
Axes of the slice: x: 2, y: 2, z: 4, core: 2. Of those that a mesh axis runs over, the one named last changes fastest.
Arguments:
- clip_tokens: bfloat16 [4, 2048, 3072], P('dp', 'ctx'), may hold values from -6 to 6
- qkv_weight: bfloat16 [3, 3072, 1536], P(None, None, 'dp'), may hold values from -0.15625 to 0.15625
- out_weight: bfloat16 [1536, 3072], P('dp'), may hold values from -0.5 to 0.5
- neighbours: int32 [32, 10], P('ctx'), may hold values from 0 to 31, as said below
- counts: int32 [32], P('ctx'), may hold values from 2 to 10, as said below
- bias_index: int32 [32, 10], P('ctx'), may hold values from 0 to 342
- rel_bias: float32 [12, 343], P('dp'), may hold values from -4 to 262
Outputs:
- layer_out: bfloat16 [4, 2048, 3072], P('dp', 'ctx')
Inputs may be any that keep to these rules, and one draw needn't show every extreme that they name: `neighbours`: tile g lies on ctx index g / 4. Row g starts with g itself; its first counts[g] entries are distinct tiles on ctx indices at most 6 away from that of g; the entries from counts[g] on equal g. Of the tiles of one ctx index, those named in the live entries of the rows of another index are at most 2, and exactly 2 for some pairs of indices. `counts`: some tile has 10 live slots.
All inputs are finite; a program needn't handle non-finite values.
Results may differ from a plain program's by a relative error of at most 0.012.
Values may be sent and summed in bfloat16 or wider, within the bound.
No kernel may reach another device: no remote copies, remote signals or barrier semaphores. Data moves between devices by JAX's collectives and lax.ppermute only.
A program may use at most 128 MiB of HBM per device.

v0:
```python
import math
import jax
import jax.numpy as jnp
from jax import lax
from jax.sharding import PartitionSpec as P

TILE = 64
REACH = 6
KMAX = 10


def shifted(value, axis, steps):
    count = lax.axis_size(axis)
    first, last = (max(0, -steps), min(count, count - steps))
    return lax.ppermute(value, axis, [(source, source + steps) for source in range(first, last)])


def local(clip_tokens, qkv_weight, out_weight, neighbours, counts, bias_index, rel_bias):
    heads_here = rel_bias.shape[0]
    width_here = out_weight.shape[0]
    head_size = width_here // heads_here
    tile_count = clip_tokens.shape[1] // TILE
    projected = jnp.einsum(
        "ctd,sdh->scth",
        lax.all_gather(clip_tokens, "dp", axis=0, tiled=True),
        qkv_weight,
        preferred_element_type=jnp.float32,
    ).astype(jnp.bfloat16)
    clip_count = projected.shape[1]
    queries = projected[0].reshape(clip_count, tile_count, TILE, heads_here, head_size)
    key_values = projected[1:3].reshape(2, clip_count, tile_count, TILE, width_here)
    own_index = lax.axis_index("ctx")
    offsets = list(range(1, REACH + 1)) + [-amount for amount in range(1, REACH + 1)]
    live_slots = jnp.arange(KMAX)[None, :] < counts[:, None]
    collected = [key_values]
    for offset in offsets:
        collected.append(shifted(key_values, "ctx", offset))
    buffer_tiles = jnp.concatenate(collected, axis=2)
    distance = own_index - neighbours // tile_count
    which_block = jnp.where(distance > 0, distance, jnp.where(distance < 0, REACH - distance, 0))
    position = which_block * tile_count + neighbours % tile_count
    gathered = jnp.take(buffer_tiles, position.reshape(-1), axis=2)
    gathered = gathered.reshape(2, clip_count, tile_count, KMAX, TILE, heads_here, head_size)
    scores = jnp.einsum(
        "ctihd,ctmjhd->cthimj", queries, gathered[0], preferred_element_type=jnp.float32
    ) * (1.0 / math.sqrt(head_size))
    one_hot = (bias_index[:, :, None] == jnp.arange(rel_bias.shape[1])[None, None, :]).astype(
        jnp.float32
    )
    looked_up = jnp.einsum("tmr,hr->thm", one_hot, rel_bias, precision=lax.Precision.HIGHEST)
    scores = scores + looked_up[None, :, :, None, :, None]
    scores = jnp.where(live_slots[None, :, None, None, :, None], scores, -1e30)
    row_max = jnp.max(scores, axis=(4, 5), keepdims=True)
    weights = jnp.exp(scores - row_max)
    weight_sum = jnp.sum(weights, axis=(4, 5))
    blended = jnp.einsum(
        "cthimj,ctmjhd->ctihd",
        weights.astype(jnp.bfloat16),
        gathered[1],
        preferred_element_type=jnp.float32,
    )
    attended = (blended / jnp.transpose(weight_sum, (0, 1, 3, 2))[..., None]).astype(jnp.bfloat16)
    attended = attended.reshape(clip_count, tile_count * TILE, width_here)
    partial_out = jnp.einsum(
        "cth,hd->ctd", attended, out_weight, preferred_element_type=jnp.float32
    ).astype(jnp.bfloat16)
    return lax.psum_scatter(
        lax.optimization_barrier(partial_out).astype(jnp.float32).astype(jnp.bfloat16),
        "dp",
        scatter_dimension=0,
        tiled=True,
    )


def solution(mesh):
    placed = (
        P("dp", "ctx", None),
        P(None, None, "dp"),
        P("dp", None),
        P("ctx", None),
        P("ctx"),
        P("ctx", None),
        P("dp", None),
    )
    return jax.shard_map(
        local, mesh=mesh, in_specs=placed, out_specs=P("dp", "ctx", None), check_vma=False
    )
```

profile of v0, /device:TPU:0, one launch (start us, length us, event | category | flops | bytes accessed | tf_op | source)
XLA Modules:
  0.0 739.2 jit_solution(10897213490841283450)
XLA Ops:
  7.3 74.8 %all-gather.2.cloned.1.call-done = bf16[4,256,3072]{2,1,0:T(8,128)(2,1)} async-done(((bf16[1,256,3072]{2,1,0:T(8,128)(2,1)}), bf16[4,256,3072]{2,1,0:T(8,128)(2,1)}) %all-gather.2.cloned.1.call-update) | async-done | bytes 6291472 | tf_op jit(solution)/shard_map/all_gather | solution.py:25
  82.1 12.5 %convert_bitcast_fusion = bf16[3,4,256,384]{3,2,1,0:T(8,128)(2,1)S(1)} fusion(bf16[4,256,3072]{2,1,0:T(8,128)(2,1)} %all-gather.2.cloned.1.call-done, bf16[3,3072,384]{2,1,0:T(8,128)(2,1)} %param.8), kind=kOutput, calls=%fused_computation.19 | convolution fusion | flops 7248936960 | bytes 15728640 | tf_op jit(solution)/shard_map/ctd,sdh->scth/dot_general | solution.py:23
  94.6 1.4 copy-done.1
  96.0 1.3 slice.20
  97.3 2.9 collective-permute-start
  100.2 3.6 collective-permute-start.1
  103.8 4.3 collective-permute-start.2
  108.1 2.4 collective-permute-start.3
  110.5 2.5 collective-permute-start.4
  113.0 27.0 %collective-permute-start.5 = (bf16[2,4,4,64,384]{4,3,2,1,0:T(8,128)(2,1)}, bf16[2,4,4,64,384]{4,3,2,1,0:T(8,128)(2,1)}, u32[]{:S(2)}, u32[]{:S(2)}) collective-permute-start(bf16[2,4,4,64,384]{4,3,2,1,0:T(8,128)(2,1)} %bitcast.4), channel_id=1, source_target_pairs={{0,6},{1,7},{8,14},{9,15},{16,22},{17,23},{24,30},{25,31}} | collective-permute-start | bytes 4718600 | tf_op jit(solution)/shard_map/ppermute | solution.py:15
  140.0 1.3 collective-permute-start.6
  141.9 29.6 %collective-permute-done.2 = bf16[2,4,4,64,384]{4,3,2,1,0:T(8,128)(2,1)} collective-permute-done((bf16[2,4,4,64,384]{4,3,2,1,0:T(8,128)(2,1)}, bf16[2,4,4,64,384]{4,3,2,1,0:T(8,128)(2,1)}, u32[]{:S(2)}, u32[]{:S(2)}) %collective-permute-start.2) | collective-permute-done | bytes 1572896 | tf_op jit(solution)/shard_map/ppermute | solution.py:15
  171.5 1.3 collective-permute-start.7
  172.8 32.5 %collective-permute-done.3 = bf16[2,4,4,64,384]{4,3,2,1,0:T(8,128)(2,1)} collective-permute-done((bf16[2,4,4,64,384]{4,3,2,1,0:T(8,128)(2,1)}, bf16[2,4,4,64,384]{4,3,2,1,0:T(8,128)(2,1)}, u32[]{:S(2)}, u32[]{:S(2)}) %collective-permute-start.3) | collective-permute-done | bytes 1572896 | tf_op jit(solution)/shard_map/ppermute | solution.py:15
  206.6 32.3 %collective-permute-done.4 = bf16[2,4,4,64,384]{4,3,2,1,0:T(8,128)(2,1)} collective-permute-done((bf16[2,4,4,64,384]{4,3,2,1,0:T(8,128)(2,1)}, bf16[2,4,4,64,384]{4,3,2,1,0:T(8,128)(2,1)}, u32[]{:S(2)}, u32[]{:S(2)}) %collective-permute-start.4) | collective-permute-done | bytes 1572896 | tf_op jit(solution)/shard_map/ppermute | solution.py:15
  240.2 32.4 %collective-permute-done.5 = bf16[2,4,4,64,384]{4,3,2,1,0:T(8,128)(2,1)} collective-permute-done((bf16[2,4,4,64,384]{4,3,2,1,0:T(8,128)(2,1)}, bf16[2,4,4,64,384]{4,3,2,1,0:T(8,128)(2,1)}, u32[]{:S(2)}, u32[]{:S(2)}) %collective-permute-start.5) | collective-permute-done | bytes 1572896 | tf_op jit(solution)/shard_map/ppermute | solution.py:15
  273.9 2.8 constant_dynamic-update-slice_fusion.12
  276.7 2.1 slice.22
  278.8 2.4 reshape_squeeze.3
  281.2 1.3 collective-permute-start.11
  282.5 2.8 constant_dynamic-update-slice_fusion.11
  285.3 2.8 constant_dynamic-update-slice_fusion.10
  288.2 2.8 constant_dynamic-update-slice_fusion.9
  290.9 2.8 constant_dynamic-update-slice_fusion.8
  293.7 2.8 constant_dynamic-update-slice_fusion.7
  296.5 2.8 constant_dynamic-update-slice_fusion.6
  299.2 2.8 constant_dynamic-update-slice_fusion.5
  302.0 9.5 %collective-permute-done.7 = bf16[2,4,4,64,384]{4,3,2,1,0:T(8,128)(2,1)} collective-permute-done((bf16[2,4,4,64,384]{4,3,2,1,0:T(8,128)(2,1)}, bf16[2,4,4,64,384]{4,3,2,1,0:T(8,128)(2,1)}, u32[]{:S(2)}, u32[]{:S(2)}) %collective-permute-start.7) | collective-permute-done | bytes 1572896 | tf_op jit(solution)/shard_map/ppermute | solution.py:15
  311.5 2.8 constant_dynamic-update-slice_fusion.4
  314.3 66.1 %collective-permute-done.8 = bf16[2,4,4,64,384]{4,3,2,1,0:T(8,128)(2,1)} collective-permute-done((bf16[2,4,4,64,384]{4,3,2,1,0:T(8,128)(2,1)}, bf16[2,4,4,64,384]{4,3,2,1,0:T(8,128)(2,1)}, u32[]{:S(2)}, u32[]{:S(2)}) %collective-permute-start.8) | collective-permute-done | bytes 1572896 | tf_op jit(solution)/shard_map/ppermute | solution.py:15
  380.4 2.7 constant_dynamic-update-slice_fusion.3
  383.1 2.8 constant_dynamic-update-slice_fusion.2
  385.9 146.2 %collective-permute-done.10 = bf16[2,4,4,64,384]{4,3,2,1,0:T(8,128)(2,1)} collective-permute-done((bf16[2,4,4,64,384]{4,3,2,1,0:T(8,128)(2,1)}, bf16[2,4,4,64,384]{4,3,2,1,0:T(8,128)(2,1)}, u32[]{:S(2)}, u32[]{:S(2)}) %collective-permute-start.10) | collective-permute-done | bytes 1572896 | tf_op jit(solution)/shard_map/ppermute | solution.py:15
  532.1 2.7 constant_dynamic-update-slice_fusion.1
  534.8 1.3 constant_dynamic-update-slice_fusion
  536.2 15.1 %gather_fusion = bf16[40,2,4,64,384]{4,3,2,1,0:T(8,128)(2,1)} fusion(bf16[2,4,52,64,384]{4,3,2,1,0:T(8,128)(2,1)} %constant_dynamic-update-slice_fusion, s32[1024]{0:T(1024)S(1)} %pad_clamp_fusion), kind=kCustom, calls=%fused_computation | custom fusion | bytes 31457440 | tf_op jit(solution)/shard_map/jit(_take)/gather | solution.py:42
  551.3 8.4 %select_bitcast_fusion = bf16[2,4,40,64,384]{4,3,1,0,2:T(8,128)(2,1)S(1)} fusion(bf16[40,2,4,64,384]{4,3,2,1,0:T(8,128)(2,1)} %gather_fusion, pred[40]{0:T(512)(128)(4,1)S(1)} %compare_and_fusion), kind=kLoop, calls=%fused_computation.1 | loop fusion | flops 7864320 | bytes 31457320 | tf_op jit(solution)/shard_map/jit(_take)/select_n | solution.py:42
  559.7 6.3 fusion.35
  566.0 20.6 %reshape.95 = bf16[4,4,10,64,3,128]{5,4,3,0,2,1:T(4,128)(2,1)} reshape(bf16[1,4,40,64,384]{4,3,1,0,2:T(8,128)(2,1)} %get-tuple-element.6) | data formatting | bytes 15728640 | tf_op jit(solution)/shard_map/squeeze | solution.py:45
  586.6 9.4 %copy.25 = bf16[4,4,10,64,3,128]{5,3,2,4,1,0:T(8,128)(2,1)} copy(bf16[4,4,10,64,3,128]{5,4,3,0,2,1:T(4,128)(2,1)} %reshape.95) | data formatting | bytes 15728640 | tf_op jit(solution)/shard_map/squeeze | solution.py:45
  596.0 10.9 %fusion.24 = f32[4,4,3,64,640]{3,4,2,1,0} fusion(bf16[4,4,3,128,640]{3,4,2,1,0:T(8,128)(2,1)} %bitcast.55, bf16[4,4,64,3,128]{4,3,2,1,0:T(4,128)(2,1)S(1)} %reshape_squeeze.3), kind=kOutput, calls=%fused_computation.23 | convolution fusion | flops 503316480 | bytes 16515072
  606.9 8.9 %fusion.2 = f32[4,4,3,64]{3,2,1,0:T(4,128)S(1)} fusion(f32[4,4,3,64,10,64]{3,5,4,2,1,0:T(8,128)} %bitcast.52, f32[4,3,10]{2,1,0:T(4,128)S(1)} %convolution_bitcast_fusion, pred[4,10]{1,0:T(4,128)(4,1)S(1)} %iota_compare_fusion.2), kind=kLoop, calls=%fused_computation.6 | loop fusion | flops 7861248 | bytes 7877128 | tf_op jit(solution)/shard_map/reduce_max | solution.py:53
  615.8 8.0 %fusion = f32[4,4,3,64]{3,2,1,0:T(4,128)S(1)} fusion(f32[4,4,3,64,10,64]{3,5,4,2,1,0:T(8,128)} %bitcast.53, f32[4,4,3,64]{3,2,1,0:T(4,128)S(1)} %fusion.2, f32[4,3,10]{2,1,0:T(4,128)S(1)} %convolution_bitcast_fusion, pred[4,10]{1,0:T(4,128)(4,1)S(1)} %iota_compare_fusion.2), kind=kLoop, calls=%fused_computation.4 | loop fusion | flops 9827328 | bytes 7889416 | tf_op jit(solution)/shard_map/reduce_sum | solution.py:55
  623.8 20.7 %reshape.94 = bf16[4,4,10,64,3,128]{5,4,3,0,2,1:T(4,128)(2,1)} reshape(bf16[1,4,40,64,384]{4,3,1,0,2:T(8,128)(2,1)} %get-tuple-element.5) | data formatting | bytes 15728640 | tf_op jit(solution)/shard_map/squeeze | solution.py:59
  644.5 11.6 %fusion.19 = bf16[4,4,64,3,128]{4,2,3,1,0:T(8,128)(2,1)S(1)} fusion(f32[4,4,3,64,10,64]{3,5,4,2,1,0:T(8,128)} %bitcast.54, f32[4,4,3,64]{3,2,1,0:T(4,128)S(1)} %fusion.2, f32[4,3,10]{2,1,0:T(4,128)S(1)} %convolution_bitcast_fusion, pred[4,10]{1,0:T(4,128)(4,1)S(1)} %iota_compare_fusion.2, bf16[4,4,10,64,3,128]{5,4,3,0,2,1:T(4,128)(2,1)} %reshape.94, ...), kind=kOutput, calls=%fused_computation.21 | convolution fusion | flops 513933312 | bytes 16540168 | tf_op jit(solution)/shard_map/cthimj,ctmjhd->ctihd/dot_general | solution.py:56
  656.7 1.4 reshape.78
  658.2 6.5 convolution_convert_fusion
  664.7 67.6 %reduce-scatter.4.cloned.1.call-done = bf16[1,256,3072]{2,1,0:T(8,128)(2,1)} async-done(((bf16[4,256,3072]{2,1,0:T(8,128)(2,1)}), bf16[1,256,3072]{2,1,0:T(8,128)(2,1)}) %reduce-scatter.4.cloned.1.call-update) | async-done | bytes 1572880
  (32 shorter events, 6.0 us)
Async XLA Ops:
  6.5 651.7 %copy-start = (bf16[384,3072]{1,0:T(8,128)(2,1)S(1)}, bf16[384,3072]{1,0:T(8,128)(2,1)}, u32[]{:S(2)}) copy-start(bf16[384,3072]{1,0:T(8,128)(2,1)} %param.9) | copy-start | bytes 7077892
  6.5 75.6 %all-gather.2.cloned.1.call-start = ((), (), s32[]{:S(2)}) async-start(), calls=%async_computation.1 | async-start | bytes 7864320 | tf_op jit(solution)/shard_map/all_gather | solution.py:25
  7.3 134.0 %copy-start.2 = (s32[4,10]{1,0:T(4,128)S(1)}, s32[4,10]{1,0:T(4,128)}, u32[]{:S(2)}) copy-start(s32[4,10]{1,0:T(4,128)} %param.10) | copy-start | bytes 484
  7.3 134.2 %copy-start.3 = (f32[3,343]{1,0:T(4,128)S(1)}, f32[3,343]{1,0:T(4,128)}, u32[]{:S(2)}) copy-start(f32[3,343]{1,0:T(4,128)} %param.13) | copy-start | bytes 12352
  7.3 134.2 %copy-start.4 = (s32[4,10]{1,0:T(4,128)S(1)}, s32[4,10]{1,0:T(4,128)}, u32[]{:S(2)}) copy-start(s32[4,10]{1,0:T(4,128)} %param.12) | copy-start | bytes 484
  7.3 199.2 %copy-start.5 = (s32[4]{0:T(128)S(1)}, s32[4]{0:T(128)}, u32[]{:S(2)}) copy-start(s32[4]{0:T(128)} %param.11) | copy-start | bytes 52
  7.3 725.0 %reduce-scatter.4.cloned.1.call-start = ((), (), s32[]{:S(2)}) async-start(), calls=%async_computation.2 | async-start | bytes 7864320
  94.6 1.4 copy-start.1
  97.3 15.7 %collective-permute-start = (bf16[2,4,4,64,384]{4,3,2,1,0:T(8,128)(2,1)}, bf16[2,4,4,64,384]{4,3,2,1,0:T(8,128)(2,1)}, u32[]{:S(2)}, u32[]{:S(2)}) collective-permute-start(bf16[2,4,4,64,384]{4,3,2,1,0:T(8,128)(2,1)} %bitcast.4), channel_id=1, source_target_pairs={{0,1},{1,2},{2,3},{3,4},{4,5},{5,6},{6,7},{8,9},{9,10},{10,11},{11... | collective-permute-start | bytes 4718600 | tf_op jit(solution)/shard_map/ppermute | solution.py:15
  100.2 39.8 %collective-permute-start.1 = (bf16[2,4,4,64,384]{4,3,2,1,0:T(8,128)(2,1)}, bf16[2,4,4,64,384]{4,3,2,1,0:T(8,128)(2,1)}, u32[]{:S(2)}, u32[]{:S(2)}) collective-permute-start(bf16[2,4,4,64,384]{4,3,2,1,0:T(8,128)(2,1)} %bitcast.4), channel_id=1, source_target_pairs={{0,2},{1,3},{2,4},{3,5},{4,6},{5,7},{8,10},{9,11},{10,12},{11,13},... | collective-permute-start | bytes 4718600 | tf_op jit(solution)/shard_map/ppermute | solution.py:15
  103.8 67.7 %collective-permute-start.2 = (bf16[2,4,4,64,384]{4,3,2,1,0:T(8,128)(2,1)}, bf16[2,4,4,64,384]{4,3,2,1,0:T(8,128)(2,1)}, u32[]{:S(2)}, u32[]{:S(2)}) collective-permute-start(bf16[2,4,4,64,384]{4,3,2,1,0:T(8,128)(2,1)} %bitcast.4), channel_id=1, source_target_pairs={{0,3},{1,4},{2,5},{3,6},{4,7},{8,11},{9,12},{10,13},{11,14},{12,15... | collective-permute-start | bytes 4718600 | tf_op jit(solution)/shard_map/ppermute | solution.py:15
  108.1 97.2 %collective-permute-start.3 = (bf16[2,4,4,64,384]{4,3,2,1,0:T(8,128)(2,1)}, bf16[2,4,4,64,384]{4,3,2,1,0:T(8,128)(2,1)}, u32[]{:S(2)}, u32[]{:S(2)}) collective-permute-start(bf16[2,4,4,64,384]{4,3,2,1,0:T(8,128)(2,1)} %bitcast.4), channel_id=1, source_target_pairs={{0,4},{1,5},{2,6},{3,7},{8,12},{9,13},{10,14},{11,15},{16,20},{17,... | collective-permute-start | bytes 4718600 | tf_op jit(solution)/shard_map/ppermute | solution.py:15
  110.5 128.4 %collective-permute-start.4 = (bf16[2,4,4,64,384]{4,3,2,1,0:T(8,128)(2,1)}, bf16[2,4,4,64,384]{4,3,2,1,0:T(8,128)(2,1)}, u32[]{:S(2)}, u32[]{:S(2)}) collective-permute-start(bf16[2,4,4,64,384]{4,3,2,1,0:T(8,128)(2,1)} %bitcast.4), channel_id=1, source_target_pairs={{0,5},{1,6},{2,7},{8,13},{9,14},{10,15},{16,21},{17,22},{18,23},{2... | collective-permute-start | bytes 4718600 | tf_op jit(solution)/shard_map/ppermute | solution.py:15
  113.0 159.7 %collective-permute-start.5 = (bf16[2,4,4,64,384]{4,3,2,1,0:T(8,128)(2,1)}, bf16[2,4,4,64,384]{4,3,2,1,0:T(8,128)(2,1)}, u32[]{:S(2)}, u32[]{:S(2)}) collective-permute-start(bf16[2,4,4,64,384]{4,3,2,1,0:T(8,128)(2,1)} %bitcast.4), channel_id=1, source_target_pairs={{0,6},{1,7},{8,14},{9,15},{16,22},{17,23},{24,30},{25,31}} | collective-permute-start | bytes 4718600 | tf_op jit(solution)/shard_map/ppermute | solution.py:15
  140.0 141.2 %collective-permute-start.6 = (bf16[2,4,4,64,384]{4,3,2,1,0:T(8,128)(2,1)}, bf16[2,4,4,64,384]{4,3,2,1,0:T(8,128)(2,1)}, u32[]{:S(2)}, u32[]{:S(2)}) collective-permute-start(bf16[2,4,4,64,384]{4,3,2,1,0:T(8,128)(2,1)} %bitcast.4), channel_id=1, source_target_pairs={{1,0},{2,1},{3,2},{4,3},{5,4},{6,5},{7,6},{9,8},{10,9},{11,10},{12... | collective-permute-start | bytes 4718600 | tf_op jit(solution)/shard_map/ppermute | solution.py:15
  171.5 140.1 %collective-permute-start.7 = (bf16[2,4,4,64,384]{4,3,2,1,0:T(8,128)(2,1)}, bf16[2,4,4,64,384]{4,3,2,1,0:T(8,128)(2,1)}, u32[]{:S(2)}, u32[]{:S(2)}) collective-permute-start(bf16[2,4,4,64,384]{4,3,2,1,0:T(8,128)(2,1)} %bitcast.4), channel_id=1, source_target_pairs={{2,0},{3,1},{4,2},{5,3},{6,4},{7,5},{10,8},{11,9},{12,10},{13,11},... | collective-permute-start | bytes 4718600 | tf_op jit(solution)/shard_map/ppermute | solution.py:15
  205.2 175.2 %collective-permute-start.8 = (bf16[2,4,4,64,384]{4,3,2,1,0:T(8,128)(2,1)}, bf16[2,4,4,64,384]{4,3,2,1,0:T(8,128)(2,1)}, u32[]{:S(2)}, u32[]{:S(2)}) collective-permute-start(bf16[2,4,4,64,384]{4,3,2,1,0:T(8,128)(2,1)} %bitcast.4), channel_id=1, source_target_pairs={{3,0},{4,1},{5,2},{6,3},{7,4},{11,8},{12,9},{13,10},{14,11},{15,12... | collective-permute-start | bytes 4718600 | tf_op jit(solution)/shard_map/ppermute | solution.py:15
  238.9 144.2 %collective-permute-start.9 = (bf16[2,4,4,64,384]{4,3,2,1,0:T(8,128)(2,1)}, bf16[2,4,4,64,384]{4,3,2,1,0:T(8,128)(2,1)}, u32[]{:S(2)}, u32[]{:S(2)}) collective-permute-start(bf16[2,4,4,64,384]{4,3,2,1,0:T(8,128)(2,1)} %bitcast.4), channel_id=1, source_target_pairs={{4,0},{5,1},{6,2},{7,3},{12,8},{13,9},{14,10},{15,11},{20,16},{21,... | collective-permute-start | bytes 4718600 | tf_op jit(solution)/shard_map/ppermute | solution.py:15
  272.6 259.4 %collective-permute-start.10 = (bf16[2,4,4,64,384]{4,3,2,1,0:T(8,128)(2,1)}, bf16[2,4,4,64,384]{4,3,2,1,0:T(8,128)(2,1)}, u32[]{:S(2)}, u32[]{:S(2)}) collective-permute-start(bf16[2,4,4,64,384]{4,3,2,1,0:T(8,128)(2,1)} %bitcast.4), channel_id=1, source_target_pairs={{5,0},{6,1},{7,2},{13,8},{14,9},{15,10},{21,16},{22,17},{23,18},{2... | collective-permute-start | bytes 4718600 | tf_op jit(solution)/shard_map/ppermute | solution.py:15
  281.2 253.6 %collective-permute-start.11 = (bf16[2,4,4,64,384]{4,3,2,1,0:T(8,128)(2,1)}, bf16[2,4,4,64,384]{4,3,2,1,0:T(8,128)(2,1)S(1)}, u32[]{:S(2)}, u32[]{:S(2)}) collective-permute-start(bf16[2,4,4,64,384]{4,3,2,1,0:T(8,128)(2,1)} %bitcast.4), channel_id=1, source_target_pairs={{6,0},{7,1},{14,8},{15,9},{22,16},{23,17},{30,24},{31,25}} | collective-permute-start | bytes 4718600 | tf_op jit(solution)/shard_map/ppermute | solution.py:15
Sparse Core Ops, SparseCore 0:
  9.2 72.8 all-gather.1
  664.9 67.4 reduce-scatter.3
where the time goes:
time: 741 us; the launch traced here: 739 us
  waiting for transfers between devices  492 us (66%)
  local copies, waits for them, and re-layouts  116 us (16%)
  starting transfers between devices  50.4 us (7%)
  matrix products  41.9 us (6%)
  other arithmetic  25.4 us (3%)
  between operations  13.6 us (2%)
    ppermute x12, waiting for transfers between devices, shifted(): lax.ppermute(value, axis, [(source, source + steps) for source in range(f...  349 us
    all_gather x1, waiting for transfers between devices, local(): lax.all_gather(clip_tokens, 'dp', axis=0, tiled=True)  74.8 us
    unnamed x3, waiting for transfers between devices  68.3 us
    ppermute x12, starting transfers between devices, shifted(): lax.ppermute(value, axis, [(source, source + steps) for source in range(f...  50.4 us
    unnamed x24, local copies, waits for them, and re-layouts  34.7 us
    squeeze x2, local copies, waits for them, and re-layouts, local(): gathered[0]  30 us
    squeeze x1, local copies, waits for them, and re-layouts, local(): gathered[1]  20.7 us
    gather x1, local copies, waits for them, and re-layouts, local(): gathered = jnp.take(buffer_tiles, position.reshape(-1), axis=2)  15.1 us
  transfers between devices with their start and end apart: 14, of which 9 were waited for; matrix products, arithmetic and copies ran while one was open for 5% of the time, Pallas kernels for 0%

commit v1 on v0

--- a/solution.py
+++ b/solution.py
@@ -7,6 +7,28 @@
 TILE = 64
 REACH = 6
 KMAX = 10
+
+
+def in_order(blocks, dim):
+    blocks = jnp.moveaxis(blocks, 0, dim)
+    lengths = blocks.shape
+    return blocks.reshape(*lengths[:dim], lengths[dim] * lengths[dim + 1], *lengths[dim + 2 :])
+
+
+def collect(x, axis, dim):
+    size = lax.axis_size(axis)
+    pairs = [(i, (i + 1) % size) for i in range(size)]
+    back = [(b, a) for a, b in pairs]
+    lower, upper = ([], [])
+    for turn in range(size - 1):
+        if turn % 2 == 0:
+            lower.append(lax.ppermute(lower[-1] if lower else x, axis, pairs))
+        else:
+            upper.append(lax.ppermute(upper[-1] if upper else x, axis, back))
+    parts = jnp.stack([*lower[::-1], x, *upper])
+    shift = lax.axis_index(axis) - len(lower)
+    parts = parts[(jnp.arange(size) - shift) % size]
+    return in_order(parts, dim)
 
 
 def shifted(value, axis, steps):
@@ -22,7 +44,7 @@
     tile_count = clip_tokens.shape[1] // TILE
     projected = jnp.einsum(
         "ctd,sdh->scth",
-        lax.all_gather(clip_tokens, "dp", axis=0, tiled=True),
+        collect(clip_tokens, "dp", 0),
         qkv_weight,
         preferred_element_type=jnp.float32,
     ).astype(jnp.bfloat16)

time: 741 us -> 785 us (1.059)
  waiting for transfers between devices: 492 us -> 520 us
    ppermute x0 -> x3, waiting for transfers between devices: none -> 101 us  [the longest x2 67.8 us: collect(): lower.append(lax.ppermute(lower[-1] if lower else x, axis, pairs))]
    all_gather x1 -> x0, waiting for transfers between devices: 74.8 us -> none  [local(): lax.all_gather(clip_tokens, 'dp', axis=0, tiled=True)]
    unnamed x24 -> x23, local copies, waits for them, and re-layouts: 34.7 us -> 30.4 us
    unnamed x3 -> x2, waiting for transfers between devices: 68.3 us -> 67.7 us
  transfers between devices with their start and end apart: 14 -> 16, of which waited for: 9 -> 11; matrix products, arithmetic and copies ran while one was open for 5% -> 5% of each run, Pallas kernels for 0% -> 0%
where the time goes in v1:
time: 785 us; the launch traced here: 783 us
  waiting for transfers between devices  520 us (66%)
  local copies, waits for them, and re-layouts  119 us (15%)
  starting transfers between devices  55.9 us (7%)
  matrix products  41.8 us (5%)
  other arithmetic  32 us (4%)
  between operations  13.6 us (2%)
    ppermute x12, waiting for transfers between devices, shifted(): lax.ppermute(value, axis, [(source, source + steps) for source in range(f...  351 us
    ppermute x2, waiting for transfers between devices, collect(): lower.append(lax.ppermute(lower[-1] if lower else x, axis, pairs))  67.8 us
    unnamed x2, waiting for transfers between devices  67.7 us
    ppermute x12, starting transfers between devices, shifted(): lax.ppermute(value, axis, [(source, source + steps) for source in range(f...  50.9 us
    ppermute x1, waiting for transfers between devices, collect(): upper.append(lax.ppermute(upper[-1] if upper else x, axis, back))  33.1 us
    unnamed x23, local copies, waits for them, and re-layouts  30.4 us
    squeeze x2, local copies, waits for them, and re-layouts, local(): gathered[0]  30 us
    squeeze x1, local copies, waits for them, and re-layouts, local(): gathered[1]  20.6 us
  transfers between devices with their start and end apart: 16, of which 11 were waited for; matrix products, arithmetic and copies ran while one was open for 5% of the time, Pallas kernels for 0%

profile of v1, /device:TPU:0, one launch (start us, length us, event | category | flops | bytes accessed | tf_op | source)
XLA Modules:
  0.0 782.6 jit_solution(6514735494726844025)
XLA Ops:
  6.5 2.9 collective-permute-start
  10.4 35.5 %collective-permute-done = bf16[1,256,3072]{2,1,0:T(8,128)(2,1)} collective-permute-done((bf16[1,256,3072]{2,1,0:T(8,128)(2,1)}, bf16[1,256,3072]{2,1,0:T(8,128)(2,1)}, u32[]{:S(2)}, u32[]{:S(2)}) %collective-permute-start) | collective-permute-done | bytes 1572896 | tf_op jit(solution)/shard_map/ppermute | solution.py:25
  47.1 33.1 %collective-permute-done.2 = bf16[1,256,3072]{2,1,0:T(8,128)(2,1)} collective-permute-done((bf16[1,256,3072]{2,1,0:T(8,128)(2,1)}, bf16[1,256,3072]{2,1,0:T(8,128)(2,1)}, u32[]{:S(2)}, u32[]{:S(2)}) %collective-permute-start.2) | collective-permute-done | bytes 1572896 | tf_op jit(solution)/shard_map/ppermute | solution.py:27
  80.2 32.3 %collective-permute-done.1 = bf16[1,256,3072]{2,1,0:T(8,128)(2,1)} collective-permute-done((bf16[1,256,3072]{2,1,0:T(8,128)(2,1)}, bf16[1,256,3072]{2,1,0:T(8,128)(2,1)}, u32[]{:S(2)}, u32[]{:S(2)}) %collective-permute-start.1) | collective-permute-done | bytes 1572896 | tf_op jit(solution)/shard_map/ppermute | solution.py:25
  112.6 6.5 maximum_bitcast_fusion
  119.1 6.4 gather_fusion
  125.5 12.4 %convert_bitcast_fusion = bf16[3,4,256,384]{3,2,0,1:T(8,128)(2,1)S(1)} fusion(bf16[3,3072,384]{2,1,0:T(8,128)(2,1)} %param.8, bf16[4,256,3072]{2,1,0:T(8,128)(2,1)} %gather_fusion), kind=kOutput, calls=%fused_computation.21 | convolution fusion | flops 7248936960 | bytes 15728640 | tf_op jit(solution)/shard_map/ctd,sdh->scth/dot_general | solution.py:45
  138.2 2.2 fusion.38
  140.4 2.4 collective-permute-start.3
  142.8 4.3 collective-permute-start.4
  147.1 4.5 collective-permute-start.5
  151.6 2.4 collective-permute-start.6
  154.1 2.5 collective-permute-start.7
  156.5 27.0 %collective-permute-start.8 = (bf16[2,4,4,64,384]{4,3,2,1,0:T(8,128)(2,1)}, bf16[2,4,4,64,384]{4,3,2,1,0:T(8,128)(2,1)}, u32[]{:S(2)}, u32[]{:S(2)}) collective-permute-start(bf16[2,4,4,64,384]{4,3,2,1,0:T(8,128)(2,1)} %get-tuple-element.7), channel_id=1, source_target_pairs={{0,6},{1,7},{8,14},{9,15},{16,22},{17,23},{24,30},{25,31}} | collective-permute-start | bytes 4718600 | tf_op jit(solution)/shard_map/ppermute | solution.py:37
  185.5 29.4 %collective-permute-done.5 = bf16[2,4,4,64,384]{4,3,2,1,0:T(8,128)(2,1)} collective-permute-done((bf16[2,4,4,64,384]{4,3,2,1,0:T(8,128)(2,1)}, bf16[2,4,4,64,384]{4,3,2,1,0:T(8,128)(2,1)}, u32[]{:S(2)}, u32[]{:S(2)}) %collective-permute-start.5) | collective-permute-done | bytes 1572896 | tf_op jit(solution)/shard_map/ppermute | solution.py:37
  216.1 32.5 %collective-permute-done.6 = bf16[2,4,4,64,384]{4,3,2,1,0:T(8,128)(2,1)} collective-permute-done((bf16[2,4,4,64,384]{4,3,2,1,0:T(8,128)(2,1)}, bf16[2,4,4,64,384]{4,3,2,1,0:T(8,128)(2,1)}, u32[]{:S(2)}, u32[]{:S(2)}) %collective-permute-start.6) | collective-permute-done | bytes 1572896 | tf_op jit(solution)/shard_map/ppermute | solution.py:37
  249.9 32.4 %collective-permute-done.7 = bf16[2,4,4,64,384]{4,3,2,1,0:T(8,128)(2,1)} collective-permute-done((bf16[2,4,4,64,384]{4,3,2,1,0:T(8,128)(2,1)}, bf16[2,4,4,64,384]{4,3,2,1,0:T(8,128)(2,1)}, u32[]{:S(2)}, u32[]{:S(2)}) %collective-permute-start.7) | collective-permute-done | bytes 1572896 | tf_op jit(solution)/shard_map/ppermute | solution.py:37
  283.7 32.3 %collective-permute-done.8 = bf16[2,4,4,64,384]{4,3,2,1,0:T(8,128)(2,1)} collective-permute-done((bf16[2,4,4,64,384]{4,3,2,1,0:T(8,128)(2,1)}, bf16[2,4,4,64,384]{4,3,2,1,0:T(8,128)(2,1)}, u32[]{:S(2)}, u32[]{:S(2)}) %collective-permute-start.8) | collective-permute-done | bytes 1572896 | tf_op jit(solution)/shard_map/ppermute | solution.py:37
  317.3 2.1 slice.24
  319.4 2.4 reshape_squeeze.3
  323.1 2.8 constant_dynamic-update-slice_fusion.11
  325.9 2.8 constant_dynamic-update-slice_fusion.10
  328.7 2.8 constant_dynamic-update-slice_fusion.9
  331.5 2.8 constant_dynamic-update-slice_fusion.8
  334.2 2.8 constant_dynamic-update-slice_fusion.7
  337.0 2.7 constant_dynamic-update-slice_fusion.6
  339.7 2.8 constant_dynamic-update-slice_fusion.5
  342.5 12.5 %collective-permute-done.10 = bf16[2,4,4,64,384]{4,3,2,1,0:T(8,128)(2,1)} collective-permute-done((bf16[2,4,4,64,384]{4,3,2,1,0:T(8,128)(2,1)}, bf16[2,4,4,64,384]{4,3,2,1,0:T(8,128)(2,1)}, u32[]{:S(2)}, u32[]{:S(2)}) %collective-permute-start.10) | collective-permute-done | bytes 1572896 | tf_op jit(solution)/shard_map/ppermute | solution.py:37
  355.0 2.7 constant_dynamic-update-slice_fusion.4
  357.7 66.1 %collective-permute-done.11 = bf16[2,4,4,64,384]{4,3,2,1,0:T(8,128)(2,1)} collective-permute-done((bf16[2,4,4,64,384]{4,3,2,1,0:T(8,128)(2,1)}, bf16[2,4,4,64,384]{4,3,2,1,0:T(8,128)(2,1)}, u32[]{:S(2)}, u32[]{:S(2)}) %collective-permute-start.11) | collective-permute-done | bytes 1572896 | tf_op jit(solution)/shard_map/ppermute | solution.py:37
  423.9 2.7 constant_dynamic-update-slice_fusion.3
  426.6 2.7 constant_dynamic-update-slice_fusion.2
  429.3 146.2 %collective-permute-done.13 = bf16[2,4,4,64,384]{4,3,2,1,0:T(8,128)(2,1)} collective-permute-done((bf16[2,4,4,64,384]{4,3,2,1,0:T(8,128)(2,1)}, bf16[2,4,4,64,384]{4,3,2,1,0:T(8,128)(2,1)}, u32[]{:S(2)}, u32[]{:S(2)}) %collective-permute-start.13) | collective-permute-done | bytes 1572896 | tf_op jit(solution)/shard_map/ppermute | solution.py:37
  575.5 2.7 constant_dynamic-update-slice_fusion.1
  578.3 1.3 constant_dynamic-update-slice_fusion
  579.6 15.1 %gather_fusion.1 = bf16[40,2,4,64,384]{4,3,2,1,0:T(8,128)(2,1)} fusion(bf16[2,4,52,64,384]{4,3,2,1,0:T(8,128)(2,1)} %constant_dynamic-update-slice_fusion, s32[1024]{0:T(1024)S(1)} %pad_clamp_fusion), kind=kCustom, calls=%fused_computation.1 | custom fusion | bytes 31457440 | tf_op jit(solution)/shard_map/jit(_take)/gather | solution.py:64
  594.7 8.4 %select_bitcast_fusion = bf16[2,4,40,64,384]{4,3,1,0,2:T(8,128)(2,1)S(1)} fusion(bf16[40,2,4,64,384]{4,3,2,1,0:T(8,128)(2,1)} %gather_fusion.1, pred[40]{0:T(512)(128)(4,1)S(1)} %compare_and_fusion), kind=kLoop, calls=%fused_computation.2 | loop fusion | flops 7864320 | bytes 31457320 | tf_op jit(solution)/shard_map/jit(_take)/select_n | solution.py:64
  603.1 6.3 fusion.37
  609.4 20.6 %reshape.159 = bf16[4,4,10,64,3,128]{5,4,3,0,2,1:T(4,128)(2,1)} reshape(bf16[1,4,40,64,384]{4,3,1,0,2:T(8,128)(2,1)} %get-tuple-element.6) | data formatting | bytes 15728640 | tf_op jit(solution)/shard_map/squeeze | solution.py:67
  630.0 9.4 %copy.51 = bf16[4,4,10,64,3,128]{5,3,2,4,1,0:T(8,128)(2,1)} copy(bf16[4,4,10,64,3,128]{5,4,3,0,2,1:T(4,128)(2,1)} %reshape.159) | data formatting | bytes 15728640 | tf_op jit(solution)/shard_map/squeeze | solution.py:67
  639.4 10.9 %fusion.24 = f32[4,4,3,64,640]{3,4,2,1,0} fusion(bf16[4,4,3,128,640]{3,4,2,1,0:T(8,128)(2,1)} %bitcast.65, bf16[4,4,64,3,128]{4,3,2,1,0:T(4,128)(2,1)S(1)} %reshape_squeeze.3), kind=kOutput, calls=%fused_computation.25 | convolution fusion | flops 503316480 | bytes 16515072
  650.4 8.9 %fusion.2 = f32[4,4,3,64]{3,2,1,0:T(4,128)S(1)} fusion(f32[4,4,3,64,10,64]{3,5,4,2,1,0:T(8,128)} %bitcast.62, f32[4,3,10]{2,1,0:T(4,128)S(1)} %convolution_bitcast_fusion, pred[4,10]{1,0:T(4,128)(4,1)S(1)} %iota_compare_fusion.2), kind=kLoop, calls=%fused_computation.7 | loop fusion | flops 7861248 | bytes 7877128 | tf_op jit(solution)/shard_map/reduce_max | solution.py:75
  659.3 8.0 %fusion = f32[4,4,3,64]{3,2,1,0:T(4,128)S(1)} fusion(f32[4,4,3,64,10,64]{3,5,4,2,1,0:T(8,128)} %bitcast.63, f32[4,4,3,64]{3,2,1,0:T(4,128)S(1)} %fusion.2, f32[4,3,10]{2,1,0:T(4,128)S(1)} %convolution_bitcast_fusion, pred[4,10]{1,0:T(4,128)(4,1)S(1)} %iota_compare_fusion.2), kind=kLoop, calls=%fused_computation.5 | loop fusion | flops 9827328 | bytes 7889416 | tf_op jit(solution)/shard_map/reduce_sum | solution.py:77
  667.3 20.6 %reshape.158 = bf16[4,4,10,64,3,128]{5,4,3,0,2,1:T(4,128)(2,1)} reshape(bf16[1,4,40,64,384]{4,3,1,0,2:T(8,128)(2,1)} %get-tuple-element.5) | data formatting | bytes 15728640 | tf_op jit(solution)/shard_map/squeeze | solution.py:81
  687.9 11.6 %fusion.19 = bf16[4,4,64,3,128]{4,2,3,1,0:T(8,128)(2,1)S(1)} fusion(f32[4,4,3,64,10,64]{3,5,4,2,1,0:T(8,128)} %bitcast.64, f32[4,4,3,64]{3,2,1,0:T(4,128)S(1)} %fusion.2, f32[4,3,10]{2,1,0:T(4,128)S(1)} %convolution_bitcast_fusion, pred[4,10]{1,0:T(4,128)(4,1)S(1)} %iota_compare_fusion.2, bf16[4,4,10,64,3,128]{5,4,3,0,2,1:T(4,128)(2,1)} %reshape.158, ...), kind=kOutput, calls=%fused_computation.23 | convolution fusion | flops 513933312 | bytes 16540168 | tf_op jit(solution)/shard_map/cthimj,ctmjhd->ctihd/dot_general | solution.py:78
  700.2 1.4 reshape.131
  701.6 6.5 convolution_convert_fusion
  708.1 67.7 %reduce-scatter.4.cloned.1.call-done = bf16[1,256,3072]{2,1,0:T(8,128)(2,1)} async-done(((bf16[4,256,3072]{2,1,0:T(8,128)(2,1)}), bf16[1,256,3072]{2,1,0:T(8,128)(2,1)}) %reduce-scatter.4.cloned.1.call-update) | async-done | bytes 1572880
  (39 shorter events, 11.4 us)
Async XLA Ops:
  6.5 695.1 %copy-start = (bf16[384,3072]{1,0:T(8,128)(2,1)S(1)}, bf16[384,3072]{1,0:T(8,128)(2,1)}, u32[]{:S(2)}) copy-start(bf16[384,3072]{1,0:T(8,128)(2,1)} %param.9) | copy-start | bytes 7077892
  6.5 769.2 %reduce-scatter.4.cloned.1.call-start = ((), (), s32[]{:S(2)}) async-start(), calls=%async_computation.1 | async-start | bytes 7864320
  6.5 39.4 %collective-permute-start = (bf16[1,256,3072]{2,1,0:T(8,128)(2,1)}, bf16[1,256,3072]{2,1,0:T(8,128)(2,1)}, u32[]{:S(2)}, u32[]{:S(2)}) collective-permute-start(bf16[1,256,3072]{2,1,0:T(8,128)(2,1)} %param.7), channel_id=1, source_target_pairs={{0,8},{8,16},{16,24},{24,0},{1,9},{9,17},{17,25},{25,1},{2,10},{10... | collective-permute-start | bytes 4718600 | tf_op jit(solution)/shard_map/ppermute | solution.py:25
  9.5 70.8 %collective-permute-start.2 = (bf16[1,256,3072]{2,1,0:T(8,128)(2,1)}, bf16[1,256,3072]{2,1,0:T(8,128)(2,1)}, u32[]{:S(2)}, u32[]{:S(2)}) collective-permute-start(bf16[1,256,3072]{2,1,0:T(8,128)(2,1)} %param.7), channel_id=1, source_target_pairs={{8,0},{16,8},{24,16},{0,24},{9,1},{17,9},{25,17},{1,25},{10,2},{18... | collective-permute-start | bytes 4718600 | tf_op jit(solution)/shard_map/ppermute | solution.py:27
  46.0 66.6 %collective-permute-start.1 = (bf16[1,256,3072]{2,1,0:T(8,128)(2,1)}, bf16[1,256,3072]{2,1,0:T(8,128)(2,1)}, u32[]{:S(2)}, u32[]{:S(2)}) collective-permute-start(bf16[1,256,3072]{2,1,0:T(8,128)(2,1)} %collective-permute-done), channel_id=1, source_target_pairs={{0,8},{8,16},{16,24},{24,0},{1,9},{9,17},{17,25},{25,1},{2,10},{10... | collective-permute-start | bytes 4718600 | tf_op jit(solution)/shard_map/ppermute | solution.py:25
  137.9 2.5 copy-start.1
  137.9 46.9 %copy-start.2 = (s32[4,10]{1,0:T(4,128)S(1)}, s32[4,10]{1,0:T(4,128)}, u32[]{:S(2)}) copy-start(s32[4,10]{1,0:T(4,128)} %param.10) | copy-start | bytes 484
  137.9 47.1 %copy-start.3 = (f32[3,343]{1,0:T(4,128)S(1)}, f32[3,343]{1,0:T(4,128)}, u32[]{:S(2)}) copy-start(f32[3,343]{1,0:T(4,128)} %param.13) | copy-start | bytes 12352
  137.9 47.1 %copy-start.4 = (s32[4,10]{1,0:T(4,128)S(1)}, s32[4,10]{1,0:T(4,128)}, u32[]{:S(2)}) copy-start(s32[4,10]{1,0:T(4,128)} %param.12) | copy-start | bytes 484
  138.0 145.6 %copy-start.5 = (s32[4]{0:T(128)S(1)}, s32[4]{0:T(128)}, u32[]{:S(2)}) copy-start(s32[4]{0:T(128)} %param.11) | copy-start | bytes 52
  140.4 16.1 %collective-permute-start.3 = (bf16[2,4,4,64,384]{4,3,2,1,0:T(8,128)(2,1)}, bf16[2,4,4,64,384]{4,3,2,1,0:T(8,128)(2,1)}, u32[]{:S(2)}, u32[]{:S(2)}) collective-permute-start(bf16[2,4,4,64,384]{4,3,2,1,0:T(8,128)(2,1)} %get-tuple-element.7), channel_id=1, source_target_pairs={{0,1},{1,2},{2,3},{3,4},{4,5},{5,6},{6,7},{8,9},{9,10},{10,11},{11... | collective-permute-start | bytes 4718600 | tf_op jit(solution)/shard_map/ppermute | solution.py:37
  142.8 40.7 %collective-permute-start.4 = (bf16[2,4,4,64,384]{4,3,2,1,0:T(8,128)(2,1)}, bf16[2,4,4,64,384]{4,3,2,1,0:T(8,128)(2,1)}, u32[]{:S(2)}, u32[]{:S(2)}) collective-permute-start(bf16[2,4,4,64,384]{4,3,2,1,0:T(8,128)(2,1)} %get-tuple-element.7), channel_id=1, source_target_pairs={{0,2},{1,3},{2,4},{3,5},{4,6},{5,7},{8,10},{9,11},{10,12},{11,13},... | collective-permute-start | bytes 4718600 | tf_op jit(solution)/shard_map/ppermute | solution.py:37
  147.1 67.7 %collective-permute-start.5 = (bf16[2,4,4,64,384]{4,3,2,1,0:T(8,128)(2,1)}, bf16[2,4,4,64,384]{4,3,2,1,0:T(8,128)(2,1)}, u32[]{:S(2)}, u32[]{:S(2)}) collective-permute-start(bf16[2,4,4,64,384]{4,3,2,1,0:T(8,128)(2,1)} %get-tuple-element.7), channel_id=1, source_target_pairs={{0,3},{1,4},{2,5},{3,6},{4,7},{8,11},{9,12},{10,13},{11,14},{12,15... | collective-permute-start | bytes 4718600 | tf_op jit(solution)/shard_map/ppermute | solution.py:37
  151.6 97.0 %collective-permute-start.6 = (bf16[2,4,4,64,384]{4,3,2,1,0:T(8,128)(2,1)}, bf16[2,4,4,64,384]{4,3,2,1,0:T(8,128)(2,1)}, u32[]{:S(2)}, u32[]{:S(2)}) collective-permute-start(bf16[2,4,4,64,384]{4,3,2,1,0:T(8,128)(2,1)} %get-tuple-element.7), channel_id=1, source_target_pairs={{0,4},{1,5},{2,6},{3,7},{8,12},{9,13},{10,14},{11,15},{16,20},{17,... | collective-permute-start | bytes 4718600 | tf_op jit(solution)/shard_map/ppermute | solution.py:37
  154.1 128.2 %collective-permute-start.7 = (bf16[2,4,4,64,384]{4,3,2,1,0:T(8,128)(2,1)}, bf16[2,4,4,64,384]{4,3,2,1,0:T(8,128)(2,1)}, u32[]{:S(2)}, u32[]{:S(2)}) collective-permute-start(bf16[2,4,4,64,384]{4,3,2,1,0:T(8,128)(2,1)} %get-tuple-element.7), channel_id=1, source_target_pairs={{0,5},{1,6},{2,7},{8,13},{9,14},{10,15},{16,21},{17,22},{18,23},{2... | collective-permute-start | bytes 4718600 | tf_op jit(solution)/shard_map/ppermute | solution.py:37
  156.5 159.5 %collective-permute-start.8 = (bf16[2,4,4,64,384]{4,3,2,1,0:T(8,128)(2,1)}, bf16[2,4,4,64,384]{4,3,2,1,0:T(8,128)(2,1)}, u32[]{:S(2)}, u32[]{:S(2)}) collective-permute-start(bf16[2,4,4,64,384]{4,3,2,1,0:T(8,128)(2,1)} %get-tuple-element.7), channel_id=1, source_target_pairs={{0,6},{1,7},{8,14},{9,15},{16,22},{17,23},{24,30},{25,31}} | collective-permute-start | bytes 4718600 | tf_op jit(solution)/shard_map/ppermute | solution.py:37
  183.6 138.3 %collective-permute-start.9 = (bf16[2,4,4,64,384]{4,3,2,1,0:T(8,128)(2,1)}, bf16[2,4,4,64,384]{4,3,2,1,0:T(8,128)(2,1)}, u32[]{:S(2)}, u32[]{:S(2)}) collective-permute-start(bf16[2,4,4,64,384]{4,3,2,1,0:T(8,128)(2,1)} %get-tuple-element.7), channel_id=1, source_target_pairs={{1,0},{2,1},{3,2},{4,3},{5,4},{6,5},{7,6},{9,8},{10,9},{11,10},{12... | collective-permute-start | bytes 4718600 | tf_op jit(solution)/shard_map/ppermute | solution.py:37
  214.8 140.2 %collective-permute-start.10 = (bf16[2,4,4,64,384]{4,3,2,1,0:T(8,128)(2,1)}, bf16[2,4,4,64,384]{4,3,2,1,0:T(8,128)(2,1)}, u32[]{:S(2)}, u32[]{:S(2)}) collective-permute-start(bf16[2,4,4,64,384]{4,3,2,1,0:T(8,128)(2,1)} %get-tuple-element.7), channel_id=1, source_target_pairs={{2,0},{3,1},{4,2},{5,3},{6,4},{7,5},{10,8},{11,9},{12,10},{13,11},... | collective-permute-start | bytes 4718600 | tf_op jit(solution)/shard_map/ppermute | solution.py:37
  248.6 175.3 %collective-permute-start.11 = (bf16[2,4,4,64,384]{4,3,2,1,0:T(8,128)(2,1)}, bf16[2,4,4,64,384]{4,3,2,1,0:T(8,128)(2,1)}, u32[]{:S(2)}, u32[]{:S(2)}) collective-permute-start(bf16[2,4,4,64,384]{4,3,2,1,0:T(8,128)(2,1)} %get-tuple-element.7), channel_id=1, source_target_pairs={{3,0},{4,1},{5,2},{6,3},{7,4},{11,8},{12,9},{13,10},{14,11},{15,12... | collective-permute-start | bytes 4718600 | tf_op jit(solution)/shard_map/ppermute | solution.py:37
  282.3 144.3 %collective-permute-start.12 = (bf16[2,4,4,64,384]{4,3,2,1,0:T(8,128)(2,1)}, bf16[2,4,4,64,384]{4,3,2,1,0:T(8,128)(2,1)}, u32[]{:S(2)}, u32[]{:S(2)}) collective-permute-start(bf16[2,4,4,64,384]{4,3,2,1,0:T(8,128)(2,1)} %get-tuple-element.7), channel_id=1, source_target_pairs={{4,0},{5,1},{6,2},{7,3},{12,8},{13,9},{14,10},{15,11},{20,16},{21,... | collective-permute-start | bytes 4718600 | tf_op jit(solution)/shard_map/ppermute | solution.py:37
  316.0 259.5 %collective-permute-start.13 = (bf16[2,4,4,64,384]{4,3,2,1,0:T(8,128)(2,1)}, bf16[2,4,4,64,384]{4,3,2,1,0:T(8,128)(2,1)}, u32[]{:S(2)}, u32[]{:S(2)}) collective-permute-start(bf16[2,4,4,64,384]{4,3,2,1,0:T(8,128)(2,1)} %get-tuple-element.7), channel_id=1, source_target_pairs={{5,0},{6,1},{7,2},{13,8},{14,9},{15,10},{21,16},{22,17},{23,18},{2... | collective-permute-start | bytes 4718600 | tf_op jit(solution)/shard_map/ppermute | solution.py:37
  321.8 256.4 %collective-permute-start.14 = (bf16[2,4,4,64,384]{4,3,2,1,0:T(8,128)(2,1)}, bf16[2,4,4,64,384]{4,3,2,1,0:T(8,128)(2,1)S(1)}, u32[]{:S(2)}, u32[]{:S(2)}) collective-permute-start(bf16[2,4,4,64,384]{4,3,2,1,0:T(8,128)(2,1)} %get-tuple-element.7), channel_id=1, source_target_pairs={{6,0},{7,1},{14,8},{15,9},{22,16},{23,17},{30,24},{31,25}} | collective-permute-start | bytes 4718600 | tf_op jit(solution)/shard_map/ppermute | solution.py:37
Sparse Core Ops, SparseCore 0:
  708.2 67.5 reduce-scatter.3
